TPU v7x, 256 devices: a whole 4x4x8 slice. The times are simulated.
256 devices in a mesh: ctx: 64 (over x_hi, z, y), head: 4 (over x_lo, core).
Axes of the slice: x: 4 (x_hi: 2, x_lo: 2; x = x_hi * 2 + x_lo), y: 4, z: 8, core: 2. Of those that a mesh axis runs over, the one named last changes fastest.
Arguments:
- queries: bfloat16 [8192, 16, 128], P('ctx', 'head'), may hold values from -30 to 30
- rotated_keys: bfloat16 [8192, 8, 128], P('ctx', 'head'), may hold values from -4 to 4
- value_vectors: bfloat16 [8192, 8, 128], P('ctx', 'head'), may hold values from -6 to 6
- out_grad: bfloat16 [8192, 5376], P('ctx', 'head'), may hold values from -16 to 16
- out_proj: bfloat16 [5376, 2048], P('ctx', 'head'), may hold values from -0.125 to 0.125
- seg_ids: int32 [8192], replicated, may hold values from 0 to 15, never falling along the last dimension, each value on 1 to 4096 neighbouring positions
Outputs:
- layer_out: bfloat16 [8192, 5376], P('ctx', 'head')
- query_gradient: bfloat16 [8192, 16, 128], P('ctx', 'head')
- grad_key: bfloat16 [8192, 8, 128], P('ctx', 'head')
- grad_value: bfloat16 [8192, 8, 128], P('ctx', 'head')
- grad_proj: float32 [5376, 2048], P('ctx', 'head')
Inputs may be any that keep to these rules, and one draw needn't show every extreme that they name: `seg_ids`: segment ids never fall along the slab; every one of the 16 books holds one token or more.
All inputs are finite; a program needn't handle non-finite values.
Results may differ from a plain program's by a relative error of at most 0.025.
Values may be sent and summed in bfloat16 or wider, within the bound.
No kernel may reach another device: no remote copies, remote signals or barrier semaphores. Data moves between devices by JAX's collectives and lax.ppermute only.
A program may use at most 128 MiB of HBM per device.

v0:
```python
import jax
import jax.numpy as jnp
from jax import lax
from jax.sharding import PartitionSpec as P

WINDOW_TOKENS = 1024


def passed_along(value, axis, by):
    count = lax.axis_size(axis)
    pairs = [(i, i + by) for i in range(count) if 0 <= i + by < count]
    return lax.ppermute(value, axis, pairs)


def shards(queries, rotated_keys, value_vectors, out_grad, out_proj, seg_ids):
    logit_scale = 168.0 ** (-0.5)
    tok_rows = queries.shape[0]
    heads_query = queries.shape[1]
    heads_kv = rotated_keys.shape[1]
    head_size = queries.shape[2]
    group_size = heads_query // heads_kv
    blocks = WINDOW_TOKENS // tok_rows
    ctx_count = lax.axis_size("ctx")
    ctx_index = lax.axis_index("ctx")
    own_block = jnp.stack([rotated_keys, value_vectors])
    received = []
    for offset in range(blocks):
        received.append(passed_along(own_block, "ctx", offset + 1))
    key_value = jnp.concatenate(received[::-1] + [own_block], axis=1)
    key_row_slice = key_value[0]
    value_row_slice = key_value[1]
    first_row = ctx_index * tok_rows
    seg_padded = jnp.concatenate([jnp.full((WINDOW_TOKENS,), -1, jnp.int32), seg_ids], 0)
    key_seg = lax.dynamic_slice_in_dim(seg_padded, first_row, WINDOW_TOKENS + tok_rows, 0)
    query_seg = lax.dynamic_slice_in_dim(seg_ids, first_row, tok_rows, 0)
    query_pos = first_row + jnp.arange(tok_rows, dtype=jnp.int32)
    key_pos = first_row - WINDOW_TOKENS + jnp.arange(WINDOW_TOKENS + tok_rows, dtype=jnp.int32)
    allowed = (key_pos[None, :] <= query_pos[:, None]) & (
        query_pos[:, None] - key_pos[None, :] < WINDOW_TOKENS
    )
    allowed = allowed & (key_pos[None, :] >= 0) & (query_seg[:, None] == key_seg[None, :])
    grouped_queries = queries.reshape(tok_rows, heads_kv, group_size, head_size)
    attention_logits = logit_scale * jnp.einsum(
        "eqco,fqo->qcef", grouped_queries, key_row_slice, preferred_element_type=jnp.float32
    )
    attention_logits = jnp.where(allowed, attention_logits, -1e30)
    top_score = jnp.max(attention_logits, axis=3, keepdims=True)
    weights = jnp.where(allowed, jnp.exp(attention_logits - top_score), 0.0)
    probs = weights / jnp.sum(weights, axis=3, keepdims=True)
    probabilities_half = probs.astype(jnp.bfloat16)
    attended_output = jnp.einsum(
        "ykip,pyj->iykj", probabilities_half, value_row_slice, preferred_element_type=jnp.float32
    )
    attended_output = attended_output.astype(jnp.bfloat16).reshape(
        tok_rows, heads_query * head_size
    )
    proj_full = lax.all_gather(out_proj, "ctx", axis=0, tiled=True)
    out_partial = lax.dot_general(
        attended_output, proj_full, (((1,), (1,)), ((), ())), preferred_element_type=jnp.float32
    )
    layer_out = lax.psum_scatter(out_partial, "head", scatter_dimension=1, tiled=True).astype(
        jnp.bfloat16
    )
    grad_full = lax.all_gather(out_grad, "head", axis=1, tiled=True)
    grad_attended = jnp.dot(grad_full, proj_full, preferred_element_type=jnp.float32).astype(
        jnp.bfloat16
    )
    proj_summed = lax.psum_scatter(
        lax.dot_general(
            grad_full, attended_output, (((0,), (0,)), ((), ())), preferred_element_type=jnp.float32
        ),
        "ctx",
        scatter_dimension=0,
        tiled=True,
    )
    grad_proj = proj_summed * (ctx_count * tok_rows) ** (-0.5)
    grouped_gradient = grad_attended.reshape(tok_rows, heads_kv, group_size, head_size)
    attn_groups = attended_output.reshape(tok_rows, heads_kv, group_size, head_size)
    probability_gradient = jnp.einsum(
        "eqco,fqo->qcef", grouped_gradient, value_row_slice, preferred_element_type=jnp.float32
    )
    row_delta = jnp.sum(
        grouped_gradient.astype(jnp.float32) * attn_groups.astype(jnp.float32), axis=3
    )
    row_delta = jnp.transpose(row_delta, (1, 2, 0))[..., None]
    score_gradient = (probs * (probability_gradient - row_delta)).astype(jnp.bfloat16)
    query_gradient = logit_scale * jnp.einsum(
        "ykip,pyj->iykj", score_gradient, key_row_slice, preferred_element_type=jnp.float32
    )
    query_gradient = query_gradient.astype(jnp.bfloat16).reshape(tok_rows, heads_query, head_size)
    key_portion = logit_scale * jnp.einsum(
        "huoe,ohul->ehl", score_gradient, grouped_queries, preferred_element_type=jnp.float32
    )
    value_portion = jnp.einsum(
        "huoe,ohul->ehl", probabilities_half, grouped_gradient, preferred_element_type=jnp.float32
    )
    both_parts = jnp.stack([key_portion, value_portion])
    halo_part = both_parts[:, :WINDOW_TOKENS]
    summed = both_parts[:, WINDOW_TOKENS:]
    for offset in range(blocks):
        distance = offset + 1
        portion = halo_part[:, (blocks - distance) * tok_rows : (blocks - distance + 1) * tok_rows]
        summed = summed + passed_along(portion, "ctx", -distance)
    grad_key = summed[0].astype(jnp.bfloat16)
    grad_value = summed[1].astype(jnp.bfloat16)
    return (layer_out, query_gradient, grad_key, grad_value, grad_proj)


def solution(mesh):
    return jax.shard_map(
        shards,
        mesh=mesh,
        in_specs=(
            P("ctx", "head", None),
            P("ctx", "head", None),
            P("ctx", "head", None),
            P("ctx", "head"),
            P("ctx", "head"),
            P(),
        ),
        out_specs=(
            P("ctx", "head"),
            P("ctx", "head", None),
            P("ctx", "head", None),
            P("ctx", "head", None),
            P("ctx", "head"),
        ),
        check_vma=False,
    )
```

profile of v0, /device:TPU:8, one launch (start us, length us, event | category | flops | bytes accessed | tf_op | source)
XLA Modules:
  0.0 1003.6 jit_solution(2260992175720324510)
XLA Ops:
  7.2 0.7 all-gather.6.cloned.1.call-update
  8.0 0.9 copy_bitcast_fusion
  8.9 5.2 collective-permute-start
  14.1 6.3 collective-permute-start.1
  20.4 5.0 collective-permute-start.2
  25.3 4.3 collective-permute-start.3
  29.6 2.9 collective-permute-start.4
  32.6 0.8 dynamic_slice.6
  33.4 0.8 pad_dynamic-slice_fusion
  34.2 1.0 fusion.15
  35.2 1.5 collective-permute-start.5
  36.7 4.0 collective-permute-start.6
  40.8 4.7 collective-permute-start.7
  45.7 2.3 collective-permute-done.7
  48.1 2.5 fusion.42
  50.6 1.9 fusion.12
  52.5 97.7 %all-gather.6.cloned.1.call-done = bf16[64,84,512]{2,1,0:T(8,128)(2,1)} async-done(((bf16[1,84,512]{2,1,0:T(8,128)(2,1)}), bf16[64,84,512]{2,1,0:T(8,128)(2,1)}) %all-gather.6.cloned.1.call-update) | async-done | bytes 5505040 | tf_op jit(solution)/shard_map/all_gather | solution.py:57
  150.2 8.9 reshape.46
  159.1 15.1 %all-gather.4.cloned.1.call-done = bf16[128,5376]{0,1:T(8,128)(2,1)} async-done(((bf16[128,1344]{0,1:T(8,128)(2,1)}), bf16[128,5376]{0,1:T(8,128)(2,1)}) %all-gather.4.cloned.1.call-update) | async-done | bytes 1376272 | tf_op jit(solution)/shard_map/all_gather | solution.py:64
  174.1 3.9 convolution_convert_fusion
  178.6 5.7 fusion.45
  184.3 7.1 convolution_bitcast_fusion
  191.5 2.1 fusion.8
  193.6 0.5 fusion.10
  194.1 0.5 copy-done.3
  194.6 0.5 convolution_bitcast_fusion.2
  195.1 1.2 fusion.26
  196.8 1.4 collective-permute-start.15
  198.2 1.3 collective-permute-start.14
  199.5 1.3 collective-permute-start.13
  200.8 0.6 dynamic-slice
  202.1 1.3 collective-permute-start.12
  203.4 1.3 collective-permute-start.11
  204.7 21.4 %collective-permute-done.15 = f32[2,128,2,128]{3,1,2,0:T(8,128)S(1)} collective-permute-done((f32[2,128,2,128]{3,1,2,0:T(8,128)}, f32[2,128,2,128]{3,1,2,0:T(8,128)S(1)}, u32[]{:S(2)}, u32[]{:S(2)}) %collective-permute-start.15) | collective-permute-done | bytes 262176 | tf_op jit(solution)/shard_map/ppermute | solution.py:12
  226.1 1.3 collective-permute-start.10
  227.3 9.9 collective-permute-done.14
  237.3 1.3 collective-permute-start.9
  238.6 1.9 collective-permute-start.8
  240.5 1.8 fusion.11
  242.4 0.8 copy.55
  243.2 12.6 %collective-permute-done.10 = f32[2,128,2,128]{3,1,2,0:T(8,128)} collective-permute-done((f32[2,128,2,128]{3,1,2,0:T(8,128)}, f32[2,128,2,128]{3,1,2,0:T(8,128)}, u32[]{:S(2)}, u32[]{:S(2)}) %collective-permute-start.10) | collective-permute-done | bytes 262176 | tf_op jit(solution)/shard_map/ppermute | solution.py:12
  255.8 1.5 fusion.32
  257.3 0.7 copy.56
  258.0 0.7 copy.57
  258.7 1.9 convert_element_type.41
  260.5 734.5 %all-reduce.4.cloned.1.call-done = f32[5376,512]{0,1:T(8,128)} async-done(((f32[5376,512]{0,1:T(8,128)}), f32[5376,512]{0,1:T(8,128)}) %all-reduce.4.cloned.1.call-update) | async-done | bytes 11010064
  995.1 1.2 dynamic-slice_multiply_fusion
  996.2 0.8 copy.58
  (46 shorter events, 1.4 us)
Async XLA Ops:
  7.2 40.9 %copy-start = (bf16[128,4,128]{2,1,0:T(4,128)(2,1)S(1)}, bf16[128,4,128]{2,1,0:T(4,128)(2,1)}, u32[]{:S(2)}) copy-start(bf16[128,4,128]{2,1,0:T(4,128)(2,1)} %param.6) | copy-start | bytes 393220
  7.2 143.0 %all-gather.6.cloned.1.call-start = ((), (), s32[]{:S(2)}) async-start(), calls=%async_computation.3 | async-start | bytes 5857280 | tf_op jit(solution)/shard_map/all_gather | solution.py:57
  7.9 166.2 %all-gather.4.cloned.1.call-start = ((), (), s32[]{:S(2)}) async-start(), calls=%async_computation.2 | async-start | bytes 1720320 | tf_op jit(solution)/shard_map/all_gather | solution.py:64
  8.9 26.3 %collective-permute-start = (bf16[2,128,2,128]{3,1,2,0:T(8,128)(2,1)S(1)}, bf16[2,128,2,128]{3,1,2,0:T(8,128)(2,1)S(1)}, u32[]{:S(2)}, u32[]{:S(2)}) collective-permute-start(bf16[2,128,2,128]{3,1,2,0:T(8,128)(2,1)S(1)} %pad_maximum_fusion.1), channel_id=1, source_target_pairs={{0,32},{4,36},{8,40},{12,44},{16,48},{20,52},{24,56},{28,60},{32,6... | collective-permute-start | bytes 393224 | tf_op jit(solution)/shard_map/ppermute | solution.py:12
  14.1 22.7 %collective-permute-start.1 = (bf16[2,128,2,128]{3,1,2,0:T(8,128)(2,1)S(1)}, bf16[2,128,2,128]{3,1,2,0:T(8,128)(2,1)S(1)}, u32[]{:S(2)}, u32[]{:S(2)}) collective-permute-start(bf16[2,128,2,128]{3,1,2,0:T(8,128)(2,1)S(1)} %pad_maximum_fusion.1), channel_id=1, source_target_pairs={{0,28},{4,32},{8,36},{12,40},{16,44},{20,48},{24,52},{28,56},{32,6... | collective-permute-start | bytes 393224 | tf_op jit(solution)/shard_map/ppermute | solution.py:12
  20.4 20.5 %collective-permute-start.2 = (bf16[2,128,2,128]{3,1,2,0:T(8,128)(2,1)S(1)}, bf16[2,128,2,128]{3,1,2,0:T(8,128)(2,1)S(1)}, u32[]{:S(2)}, u32[]{:S(2)}) collective-permute-start(bf16[2,128,2,128]{3,1,2,0:T(8,128)(2,1)S(1)} %pad_maximum_fusion.1), channel_id=1, source_target_pairs={{0,24},{4,28},{8,32},{12,36},{16,40},{20,44},{24,48},{28,52},{32,5... | collective-permute-start | bytes 393224 | tf_op jit(solution)/shard_map/ppermute | solution.py:12
  25.3 20.2 %collective-permute-start.3 = (bf16[2,128,2,128]{3,1,2,0:T(8,128)(2,1)S(1)}, bf16[2,128,2,128]{3,1,2,0:T(8,128)(2,1)S(1)}, u32[]{:S(2)}, u32[]{:S(2)}) collective-permute-start(bf16[2,128,2,128]{3,1,2,0:T(8,128)(2,1)S(1)} %pad_maximum_fusion.1), channel_id=1, source_target_pairs={{0,20},{4,24},{8,28},{12,32},{16,36},{20,40},{24,44},{28,48},{32,5... | collective-permute-start | bytes 393224 | tf_op jit(solution)/shard_map/ppermute | solution.py:12
  29.6 16.0 %collective-permute-start.4 = (bf16[2,128,2,128]{3,1,2,0:T(8,128)(2,1)S(1)}, bf16[2,128,2,128]{3,1,2,0:T(8,128)(2,1)S(1)}, u32[]{:S(2)}, u32[]{:S(2)}) collective-permute-start(bf16[2,128,2,128]{3,1,2,0:T(8,128)(2,1)S(1)} %pad_maximum_fusion.1), channel_id=1, source_target_pairs={{0,16},{4,20},{8,24},{12,28},{16,32},{20,36},{24,40},{28,44},{32,4... | collective-permute-start | bytes 393224 | tf_op jit(solution)/shard_map/ppermute | solution.py:12
  32.5 226.1 %reduce-scatter.3.cloned.1.call-start = ((), (), s32[]{:S(2)}) async-start(), calls=%async_computation.1 | async-start | bytes 3440640 | tf_op jit(solution)/shard_map/reduce_scatter | solution.py:61
  35.2 10.4 %collective-permute-start.5 = (bf16[2,128,2,128]{3,1,2,0:T(8,128)(2,1)S(1)}, bf16[2,128,2,128]{3,1,2,0:T(8,128)(2,1)S(1)}, u32[]{:S(2)}, u32[]{:S(2)}) collective-permute-start(bf16[2,128,2,128]{3,1,2,0:T(8,128)(2,1)S(1)} %pad_maximum_fusion.1), channel_id=1, source_target_pairs={{0,12},{4,16},{8,20},{12,24},{16,28},{20,32},{24,36},{28,40},{32,4... | collective-permute-start | bytes 393224 | tf_op jit(solution)/shard_map/ppermute | solution.py:12
  36.7 8.9 collective-permute-start.6
  40.8 7.2 collective-permute-start.7
  48.1 143.4 %copy-start.4 = (bf16[2,1152,2,128]{3,1,2,0:T(8,128)(2,1)}, bf16[2,1152,2,128]{3,1,2,0:T(8,128)(2,1)S(1)}, u32[]{:S(2)}) copy-start(bf16[2,1152,2,128]{3,1,2,0:T(8,128)(2,1)S(1)} %constant_dynamic-update-slice_fusion) | copy-start | bytes 3538948
  184.3 810.8 %all-reduce.4.cloned.1.call-start = ((), (), s32[]{:S(2)}) async-start(), calls=%async_computation.4 | async-start | bytes 22020096
  193.6 1.0 copy-start.3
  195.1 1.7 copy-start.1
  195.1 5.7 copy-start.5
  196.8 59.0 %copy-start.2 = (f32[1,1152,2,128]{3,1,2,0:T(8,128)S(1)}, f32[1,1152,2,128]{3,1,2,0:T(8,128)}, u32[]{:S(2)}) copy-start(f32[1,1152,2,128]{3,1,2,0:T(8,128)} %copy-done.1) | copy-start | bytes 3538948
  196.8 29.2 %collective-permute-start.15 = (f32[2,128,2,128]{3,1,2,0:T(8,128)}, f32[2,128,2,128]{3,1,2,0:T(8,128)S(1)}, u32[]{:S(2)}, u32[]{:S(2)}) collective-permute-start(f32[2,128,2,128]{3,1,2,0:T(8,128)} %get-tuple-element.26), channel_id=1, source_target_pairs={{32,0},{36,4},{40,8},{44,12},{48,16},{52,20},{56,24},{60,28},{64,3... | collective-permute-start | bytes 786440 | tf_op jit(solution)/shard_map/ppermute | solution.py:12
  198.2 39.0 %collective-permute-start.14 = (f32[2,128,2,128]{3,1,2,0:T(8,128)}, f32[2,128,2,128]{3,1,2,0:T(8,128)S(1)}, u32[]{:S(2)}, u32[]{:S(2)}) collective-permute-start(f32[2,128,2,128]{3,1,2,0:T(8,128)} %get-tuple-element.27), channel_id=1, source_target_pairs={{28,0},{32,4},{36,8},{40,12},{44,16},{48,20},{52,24},{56,28},{60,3... | collective-permute-start | bytes 786440 | tf_op jit(solution)/shard_map/ppermute | solution.py:12
  199.5 39.0 %collective-permute-start.13 = (f32[2,128,2,128]{3,1,2,0:T(8,128)}, f32[2,128,2,128]{3,1,2,0:T(8,128)}, u32[]{:S(2)}, u32[]{:S(2)}) collective-permute-start(f32[2,128,2,128]{3,1,2,0:T(8,128)} %get-tuple-element.25), channel_id=1, source_target_pairs={{24,0},{28,4},{32,8},{36,12},{40,16},{44,20},{48,24},{52,28},{56,3... | collective-permute-start | bytes 786440 | tf_op jit(solution)/shard_map/ppermute | solution.py:12
  202.1 41.1 %collective-permute-start.12 = (f32[2,128,2,128]{3,1,2,0:T(8,128)}, f32[2,128,2,128]{3,1,2,0:T(8,128)}, u32[]{:S(2)}, u32[]{:S(2)}) collective-permute-start(f32[2,128,2,128]{3,1,2,0:T(8,128)} %get-tuple-element.24), channel_id=1, source_target_pairs={{20,0},{24,4},{28,8},{32,12},{36,16},{40,20},{44,24},{48,28},{52,3... | collective-permute-start | bytes 786440 | tf_op jit(solution)/shard_map/ppermute | solution.py:12
  203.4 39.8 %collective-permute-start.11 = (f32[2,128,2,128]{3,1,2,0:T(8,128)}, f32[2,128,2,128]{3,1,2,0:T(8,128)}, u32[]{:S(2)}, u32[]{:S(2)}) collective-permute-start(f32[2,128,2,128]{3,1,2,0:T(8,128)} %get-tuple-element.23), channel_id=1, source_target_pairs={{16,0},{20,4},{24,8},{28,12},{32,16},{36,20},{40,24},{44,28},{48,3... | collective-permute-start | bytes 786440 | tf_op jit(solution)/shard_map/ppermute | solution.py:12
  226.1 29.7 %collective-permute-start.10 = (f32[2,128,2,128]{3,1,2,0:T(8,128)}, f32[2,128,2,128]{3,1,2,0:T(8,128)}, u32[]{:S(2)}, u32[]{:S(2)}) collective-permute-start(f32[2,128,2,128]{3,1,2,0:T(8,128)} %get-tuple-element.22), channel_id=1, source_target_pairs={{12,0},{16,4},{20,8},{24,12},{28,16},{32,20},{36,24},{40,28},{44,3... | collective-permute-start | bytes 786440 | tf_op jit(solution)/shard_map/ppermute | solution.py:12
  237.3 18.5 %collective-permute-start.9 = (f32[2,128,2,128]{3,1,2,0:T(8,128)}, f32[2,128,2,128]{3,1,2,0:T(8,128)}, u32[]{:S(2)}, u32[]{:S(2)}) collective-permute-start(f32[2,128,2,128]{3,1,2,0:T(8,128)} %get-tuple-element.21), channel_id=1, source_target_pairs={{8,0},{12,4},{16,8},{20,12},{24,16},{28,20},{32,24},{36,28},{40,32... | collective-permute-start | bytes 786440 | tf_op jit(solution)/shard_map/ppermute | solution.py:12
  238.6 17.2 %collective-permute-start.8 = (f32[2,128,2,128]{3,1,2,0:T(8,128)S(1)}, f32[2,128,2,128]{3,1,2,0:T(8,128)}, u32[]{:S(2)}, u32[]{:S(2)}) collective-permute-start(f32[2,128,2,128]{3,1,2,0:T(8,128)S(1)} %get-tuple-element.20), channel_id=1, source_target_pairs={{4,0},{8,4},{12,8},{16,12},{20,16},{24,20},{28,24},{32,28},{36,32}... | collective-permute-start | bytes 786440 | tf_op jit(solution)/shard_map/ppermute | solution.py:12
Sparse Core Ops, SparseCore 0:
  11.6 138.4 all-gather.5
  152.0 22.0 all-gather.3
  184.4 37.1 reduce-scatter.2
  224.1 770.9 all-reduce.3
where the time goes:
time: 1000 us
  waiting for transfers between devices  894 us (89%)
  starting transfers between devices  45 us (4%)
  matrix products  24.6 us (2%)
  local copies, waits for them, and re-layouts  15.4 us (2%)
  between operations  14.9 us (1%)
    unnamed x5, waiting for transfers between devices  735 us
    all_gather x1, waiting for transfers between devices, shards(): proj_full = lax.all_gather(out_proj, 'ctx', axis=0, tiled=True)  97.7 us
    ppermute x16, waiting for transfers between devices, passed_along(): return lax.ppermute(value, axis, pairs)  46.3 us
    ppermute x16, starting transfers between devices, passed_along(): return lax.ppermute(value, axis, pairs)  44.9 us
  transfers between devices with their start and end apart: 20, of which 7 were waited for; matrix products, arithmetic and copies ran while one was open for 4% of the time, Pallas kernels for 0%

commit v1 on v0

--- a/solution.py
+++ b/solution.py
@@ -65,15 +65,15 @@
     grad_attended = jnp.dot(grad_full, proj_full, preferred_element_type=jnp.float32).astype(
         jnp.bfloat16
     )
-    proj_summed = lax.psum_scatter(
-        lax.dot_general(
-            grad_full, attended_output, (((0,), (0,)), ((), ())), preferred_element_type=jnp.float32
-        ),
-        "ctx",
-        scatter_dimension=0,
-        tiled=True,
+    proj_rows = grad_full.shape[1] // ctx_count
+    proj_partial = jnp.einsum(
+        "tcr,tj->crj",
+        grad_full.reshape(tok_rows, ctx_count, proj_rows),
+        attended_output,
+        preferred_element_type=jnp.float32,
     )
-    grad_proj = proj_summed * (ctx_count * tok_rows) ** (-0.5)
+    proj_summed = lax.psum_scatter(proj_partial, "ctx", scatter_dimension=0, tiled=True)
+    grad_proj = proj_summed.reshape(proj_rows, -1) * (ctx_count * tok_rows) ** (-0.5)
     grouped_gradient = grad_attended.reshape(tok_rows, heads_kv, group_size, head_size)
     attn_groups = attended_output.reshape(tok_rows, heads_kv, group_size, head_size)
     probability_gradient = jnp.einsum(

time: 1000 us -> 659 us (0.66); the launches traced: 1000 us -> 652 us
  waiting for transfers between devices: 894 us -> 540 us
    unnamed x5 -> x4, waiting for transfers between devices: 735 us -> 0.73 us
    reduce_scatter x0 -> x1, waiting for transfers between devices: none -> 359 us  [shards(): lax.psum_scatter(proj_partial, 'ctx', scatter_dimension=0, tiled=True)]
    ppermute x16, waiting for transfers between devices: 46.3 us -> 72.3 us  [passed_along(): return lax.ppermute(value, axis, pairs)]
  transfers between devices with their start and end apart: 20 -> 20, of which waited for: 7 -> 13; matrix products, arithmetic and copies ran while one was open for 4% -> 5% of each run, Pallas kernels for 0% -> 0%
where the time goes in v1:
time: 659 us; the launch traced here: 652 us
  waiting for transfers between devices  540 us (82%)
  starting transfers between devices  49.4 us (7%)
  matrix products  22 us (3%)
  local copies, waits for them, and re-layouts  16.8 us (3%)
  between operations  14.2 us (2%)
  other arithmetic  9.73 us (1%)
    reduce_scatter x1, waiting for transfers between devices, shards(): lax.psum_scatter(proj_partial, 'ctx', scatter_dimension=0, tiled=True)  359 us
    all_gather x1, waiting for transfers between devices, shards(): proj_full = lax.all_gather(out_proj, 'ctx', axis=0, tiled=True)  92.4 us
    ppermute x16, waiting for transfers between devices, passed_along(): return lax.ppermute(value, axis, pairs)  72.3 us
    ppermute x16, starting transfers between devices, passed_along(): return lax.ppermute(value, axis, pairs)  49.2 us
    all_gather x1, waiting for transfers between devices, shards(): grad_full = lax.all_gather(out_grad, 'head', axis=1, tiled=True)  15.1 us
  transfers between devices with their start and end apart: 20, of which 13 were waited for; matrix products, arithmetic and copies ran while one was open for 5% of the time, Pallas kernels for 0%

profile of v1, /device:TPU:8, one launch (start us, length us, event | category | flops | bytes accessed | tf_op | source)
XLA Modules:
  0.0 651.9 jit_solution(7047656950511083596)
XLA Ops:
  8.0 0.9 copy_bitcast_fusion
  8.9 3.5 collective-permute-start.7
  12.4 4.2 collective-permute-start.6
  16.6 4.3 collective-permute-start.5
  20.9 6.0 collective-permute-start.1
  26.9 5.5 collective-permute-start
  32.5 0.8 dynamic_slice.6
  33.3 0.8 pad_dynamic-slice_fusion
  34.0 1.0 fusion.15
  35.1 1.5 collective-permute-done
  36.6 6.2 collective-permute-start.2
  42.8 3.4 collective-permute-start.3
  46.3 4.6 collective-permute-start.4
  50.9 2.5 collective-permute-done.4
  53.6 2.4 fusion.42
  56.0 1.9 fusion.12
  57.9 92.4 %all-gather.6.cloned.1.call-done = bf16[64,84,512]{2,1,0:T(8,128)(2,1)} async-done(((bf16[1,84,512]{2,1,0:T(8,128)(2,1)}), bf16[64,84,512]{2,1,0:T(8,128)(2,1)}) %all-gather.6.cloned.1.call-update) | async-done | bytes 5505040 | tf_op jit(solution)/shard_map/all_gather | solution.py:57
  150.2 8.9 %reshape.53 = bf16[5376,512]{1,0:T(8,128)(2,1)} reshape(bf16[64,84,512]{2,1,0:T(8,128)(2,1)} %all-gather.6.cloned.1.call-done) | data formatting | bytes 11010048
  159.1 15.1 %all-gather.4.cloned.1.call-done = bf16[128,5376]{0,1:T(8,128)(2,1)} async-done(((bf16[128,1344]{0,1:T(8,128)(2,1)}), bf16[128,5376]{0,1:T(8,128)(2,1)}) %all-gather.4.cloned.1.call-update) | async-done | bytes 1376272 | tf_op jit(solution)/shard_map/all_gather | solution.py:64
  174.2 3.9 convolution_convert_fusion
  178.6 5.8 fusion.45
  184.5 2.2 reshape.51
  186.7 6.0 convolution_bitcast_fusion
  192.7 1.2 copy-done.4
  194.0 2.1 fusion.8
  197.1 1.1 fusion.26
  198.4 2.6 collective-permute-start.8
  201.0 1.3 collective-permute-start.9
  202.3 1.3 collective-permute-start.10
  203.6 1.3 collective-permute-start.11
  204.9 1.3 collective-permute-start.12
  206.2 2.9 collective-permute-done.8
  209.1 1.3 collective-permute-start.13
  210.4 5.3 collective-permute-done.9
  215.6 1.3 collective-permute-start.15
  216.9 9.0 %collective-permute-done.10 = f32[2,128,2,128]{3,1,2,0:T(8,128)S(1)} collective-permute-done((f32[2,128,2,128]{3,1,2,0:T(8,128)S(1)}, f32[2,128,2,128]{3,1,2,0:T(8,128)S(1)}, u32[]{:S(2)}, u32[]{:S(2)}) %collective-permute-start.10) | collective-permute-done | bytes 262176 | tf_op jit(solution)/shard_map/ppermute | solution.py:12
  225.9 1.3 collective-permute-start.14
  227.6 0.8 copy.56
  228.4 2.1 collective-permute-done.11
  230.8 3.8 collective-permute-done.13
  234.6 30.6 %collective-permute-done.15 = f32[2,128,2,128]{3,1,2,0:T(8,128)} collective-permute-done((f32[2,128,2,128]{3,1,2,0:T(8,128)}, f32[2,128,2,128]{3,1,2,0:T(8,128)}, u32[]{:S(2)}, u32[]{:S(2)}) %collective-permute-start.15) | collective-permute-done | bytes 262176 | tf_op jit(solution)/shard_map/ppermute | solution.py:12
  265.2 14.4 %collective-permute-done.14 = f32[2,128,2,128]{3,1,2,0:T(8,128)} collective-permute-done((f32[2,128,2,128]{3,1,2,0:T(8,128)S(1)}, f32[2,128,2,128]{3,1,2,0:T(8,128)}, u32[]{:S(2)}, u32[]{:S(2)}) %collective-permute-start.14) | collective-permute-done | bytes 262176 | tf_op jit(solution)/shard_map/ppermute | solution.py:12
  279.6 1.5 fusion.32
  281.1 0.7 copy.58
  281.8 0.7 copy.57
  282.5 1.9 convert_element_type.41
  284.4 359.3 %reduce-scatter.5.cloned.1.call-done = f32[1,84,512]{2,1,0:T(8,128)} async-done(((f32[64,84,512]{2,1,0:T(8,128)}), f32[1,84,512]{2,1,0:T(8,128)}) %reduce-scatter.5.cloned.1.call-update) | async-done | bytes 172048 | tf_op jit(solution)/shard_map/reduce_scatter | solution.py:75
  643.7 1.6 multiply_bitcast_fusion
  (47 shorter events, 3.6 us)
Async XLA Ops:
  7.2 46.4 %copy-start = (bf16[128,4,128]{2,1,0:T(4,128)(2,1)S(1)}, bf16[128,4,128]{2,1,0:T(4,128)(2,1)}, u32[]{:S(2)}) copy-start(bf16[128,4,128]{2,1,0:T(4,128)(2,1)} %param.6) | copy-start | bytes 393220
  7.2 143.1 %all-gather.6.cloned.1.call-start = ((), (), s32[]{:S(2)}) async-start(), calls=%async_computation.5 | async-start | bytes 5857280 | tf_op jit(solution)/shard_map/all_gather | solution.py:57
  7.9 166.3 %all-gather.4.cloned.1.call-start = ((), (), s32[]{:S(2)}) async-start(), calls=%async_computation.3 | async-start | bytes 1720320 | tf_op jit(solution)/shard_map/all_gather | solution.py:64
  8.9 44.6 %collective-permute-start.7 = (bf16[2,128,2,128]{3,1,2,0:T(8,128)(2,1)S(1)}, bf16[2,128,2,128]{3,1,2,0:T(8,128)(2,1)S(1)}, u32[]{:S(2)}, u32[]{:S(2)}) collective-permute-start(bf16[2,128,2,128]{3,1,2,0:T(8,128)(2,1)S(1)} %pad_maximum_fusion.1), channel_id=1, source_target_pairs={{0,4},{4,8},{8,12},{12,16},{16,20},{20,24},{24,28},{28,32},{32,36}... | collective-permute-start | bytes 393224 | tf_op jit(solution)/shard_map/ppermute | solution.py:12
  12.4 41.1 %collective-permute-start.6 = (bf16[2,128,2,128]{3,1,2,0:T(8,128)(2,1)S(1)}, bf16[2,128,2,128]{3,1,2,0:T(8,128)(2,1)S(1)}, u32[]{:S(2)}, u32[]{:S(2)}) collective-permute-start(bf16[2,128,2,128]{3,1,2,0:T(8,128)(2,1)S(1)} %pad_maximum_fusion.1), channel_id=1, source_target_pairs={{0,8},{4,12},{8,16},{12,20},{16,24},{20,28},{24,32},{28,36},{32,40... | collective-permute-start | bytes 393224 | tf_op jit(solution)/shard_map/ppermute | solution.py:12
  16.6 36.8 %collective-permute-start.5 = (bf16[2,128,2,128]{3,1,2,0:T(8,128)(2,1)S(1)}, bf16[2,128,2,128]{3,1,2,0:T(8,128)(2,1)S(1)}, u32[]{:S(2)}, u32[]{:S(2)}) collective-permute-start(bf16[2,128,2,128]{3,1,2,0:T(8,128)(2,1)S(1)} %pad_maximum_fusion.1), channel_id=1, source_target_pairs={{0,12},{4,16},{8,20},{12,24},{16,28},{20,32},{24,36},{28,40},{32,4... | collective-permute-start | bytes 393224 | tf_op jit(solution)/shard_map/ppermute | solution.py:12
  20.9 21.9 %collective-permute-start.1 = (bf16[2,128,2,128]{3,1,2,0:T(8,128)(2,1)S(1)}, bf16[2,128,2,128]{3,1,2,0:T(8,128)(2,1)S(1)}, u32[]{:S(2)}, u32[]{:S(2)}) collective-permute-start(bf16[2,128,2,128]{3,1,2,0:T(8,128)(2,1)S(1)} %pad_maximum_fusion.1), channel_id=1, source_target_pairs={{0,28},{4,32},{8,36},{12,40},{16,44},{20,48},{24,52},{28,56},{32,6... | collective-permute-start | bytes 393224 | tf_op jit(solution)/shard_map/ppermute | solution.py:12
  26.9 9.7 %collective-permute-start = (bf16[2,128,2,128]{3,1,2,0:T(8,128)(2,1)S(1)}, bf16[2,128,2,128]{3,1,2,0:T(8,128)(2,1)S(1)}, u32[]{:S(2)}, u32[]{:S(2)}) collective-permute-start(bf16[2,128,2,128]{3,1,2,0:T(8,128)(2,1)S(1)} %pad_maximum_fusion.1), channel_id=1, source_target_pairs={{0,32},{4,36},{8,40},{12,44},{16,48},{20,52},{24,56},{28,60},{32,6... | collective-permute-start | bytes 393224 | tf_op jit(solution)/shard_map/ppermute | solution.py:12
  32.4 250.1 %reduce-scatter.3.cloned.1.call-start = ((), (), s32[]{:S(2)}) async-start(), calls=%async_computation.2 | async-start | bytes 3440640 | tf_op jit(solution)/shard_map/reduce_scatter | solution.py:61
  36.6 9.7 %collective-permute-start.2 = (bf16[2,128,2,128]{3,1,2,0:T(8,128)(2,1)S(1)}, bf16[2,128,2,128]{3,1,2,0:T(8,128)(2,1)S(1)}, u32[]{:S(2)}, u32[]{:S(2)}) collective-permute-start(bf16[2,128,2,128]{3,1,2,0:T(8,128)(2,1)S(1)} %pad_maximum_fusion.1), channel_id=1, source_target_pairs={{0,24},{4,28},{8,32},{12,36},{16,40},{20,44},{24,48},{28,52},{32,5... | collective-permute-start | bytes 393224 | tf_op jit(solution)/shard_map/ppermute | solution.py:12
  42.8 8.0 %collective-permute-start.3 = (bf16[2,128,2,128]{3,1,2,0:T(8,128)(2,1)S(1)}, bf16[2,128,2,128]{3,1,2,0:T(8,128)(2,1)S(1)}, u32[]{:S(2)}, u32[]{:S(2)}) collective-permute-start(bf16[2,128,2,128]{3,1,2,0:T(8,128)(2,1)S(1)} %pad_maximum_fusion.1), channel_id=1, source_target_pairs={{0,20},{4,24},{8,28},{12,32},{16,36},{20,40},{24,44},{28,48},{32,5... | collective-permute-start | bytes 393224 | tf_op jit(solution)/shard_map/ppermute | solution.py:12
  46.3 7.1 %collective-permute-start.4 = (bf16[2,128,2,128]{3,1,2,0:T(8,128)(2,1)S(1)}, bf16[2,128,2,128]{3,1,2,0:T(8,128)(2,1)S(1)}, u32[]{:S(2)}, u32[]{:S(2)}) collective-permute-start(bf16[2,128,2,128]{3,1,2,0:T(8,128)(2,1)S(1)} %pad_maximum_fusion.1), channel_id=1, source_target_pairs={{0,16},{4,20},{8,24},{12,28},{16,32},{20,36},{24,40},{28,44},{32,4... | collective-permute-start | bytes 393224 | tf_op jit(solution)/shard_map/ppermute | solution.py:12
  53.6 124.7 %copy-start.3 = (bf16[2,1152,2,128]{3,1,2,0:T(8,128)(2,1)}, bf16[2,1152,2,128]{3,1,2,0:T(8,128)(2,1)S(1)}, u32[]{:S(2)}) copy-start(bf16[2,1152,2,128]{3,1,2,0:T(8,128)(2,1)S(1)} %constant_dynamic-update-slice_fusion) | copy-start | bytes 3538948
  184.4 459.3 %reduce-scatter.5.cloned.1.call-start = ((), (), s32[]{:S(2)}) async-start(), calls=%async_computation.4 | async-start | bytes 11714560 | tf_op jit(solution)/shard_map/reduce_scatter | solution.py:75
  192.7 1.3 copy-start.4
  197.1 1.4 copy-start.1
  197.1 30.1 %copy-start.5 = (bf16[2,1152,2,128]{3,1,2,0:T(8,128)(2,1)S(1)}, bf16[2,1152,2,128]{3,1,2,0:T(8,128)(2,1)}, u32[]{:S(2)}) copy-start(bf16[2,1152,2,128]{3,1,2,0:T(8,128)(2,1)} %copy-done.3) | copy-start | bytes 3538948
  198.4 81.2 %copy-start.2 = (f32[1,1152,2,128]{3,1,2,0:T(8,128)S(1)}, f32[1,1152,2,128]{3,1,2,0:T(8,128)}, u32[]{:S(2)}) copy-start(f32[1,1152,2,128]{3,1,2,0:T(8,128)} %copy-done.1) | copy-start | bytes 3538948
  198.4 10.7 %collective-permute-start.8 = (f32[2,128,2,128]{3,1,2,0:T(8,128)S(1)}, f32[2,128,2,128]{3,1,2,0:T(8,128)S(1)}, u32[]{:S(2)}, u32[]{:S(2)}) collective-permute-start(f32[2,128,2,128]{3,1,2,0:T(8,128)S(1)} %get-tuple-element.20), channel_id=1, source_target_pairs={{4,0},{8,4},{12,8},{16,12},{20,16},{24,20},{28,24},{32,28},{36,32}... | collective-permute-start | bytes 786440 | tf_op jit(solution)/shard_map/ppermute | solution.py:12
  201.0 14.6 %collective-permute-start.9 = (f32[2,128,2,128]{3,1,2,0:T(8,128)S(1)}, f32[2,128,2,128]{3,1,2,0:T(8,128)S(1)}, u32[]{:S(2)}, u32[]{:S(2)}) collective-permute-start(f32[2,128,2,128]{3,1,2,0:T(8,128)S(1)} %get-tuple-element.21), channel_id=1, source_target_pairs={{8,0},{12,4},{16,8},{20,12},{24,16},{28,20},{32,24},{36,28},{40,32... | collective-permute-start | bytes 786440 | tf_op jit(solution)/shard_map/ppermute | solution.py:12
  202.3 23.6 %collective-permute-start.10 = (f32[2,128,2,128]{3,1,2,0:T(8,128)S(1)}, f32[2,128,2,128]{3,1,2,0:T(8,128)S(1)}, u32[]{:S(2)}, u32[]{:S(2)}) collective-permute-start(f32[2,128,2,128]{3,1,2,0:T(8,128)S(1)} %get-tuple-element.22), channel_id=1, source_target_pairs={{12,0},{16,4},{20,8},{24,12},{28,16},{32,20},{36,24},{40,28},{44,3... | collective-permute-start | bytes 786440 | tf_op jit(solution)/shard_map/ppermute | solution.py:12
  203.6 26.9 %collective-permute-start.11 = (f32[2,128,2,128]{3,1,2,0:T(8,128)}, f32[2,128,2,128]{3,1,2,0:T(8,128)}, u32[]{:S(2)}, u32[]{:S(2)}) collective-permute-start(f32[2,128,2,128]{3,1,2,0:T(8,128)} %get-tuple-element.23), channel_id=1, source_target_pairs={{16,0},{20,4},{24,8},{28,12},{32,16},{36,20},{40,24},{44,28},{48,3... | collective-permute-start | bytes 786440 | tf_op jit(solution)/shard_map/ppermute | solution.py:12
  204.9 25.9 %collective-permute-start.12 = (f32[2,128,2,128]{3,1,2,0:T(8,128)}, f32[2,128,2,128]{3,1,2,0:T(8,128)}, u32[]{:S(2)}, u32[]{:S(2)}) collective-permute-start(f32[2,128,2,128]{3,1,2,0:T(8,128)} %get-tuple-element.24), channel_id=1, source_target_pairs={{20,0},{24,4},{28,8},{32,12},{36,16},{40,20},{44,24},{48,28},{52,3... | collective-permute-start | bytes 786440 | tf_op jit(solution)/shard_map/ppermute | solution.py:12
  209.1 25.5 %collective-permute-start.13 = (f32[2,128,2,128]{3,1,2,0:T(8,128)}, f32[2,128,2,128]{3,1,2,0:T(8,128)}, u32[]{:S(2)}, u32[]{:S(2)}) collective-permute-start(f32[2,128,2,128]{3,1,2,0:T(8,128)} %get-tuple-element.25), channel_id=1, source_target_pairs={{24,0},{28,4},{32,8},{36,12},{40,16},{44,20},{48,24},{52,28},{56,3... | collective-permute-start | bytes 786440 | tf_op jit(solution)/shard_map/ppermute | solution.py:12
  215.6 49.6 %collective-permute-start.15 = (f32[2,128,2,128]{3,1,2,0:T(8,128)}, f32[2,128,2,128]{3,1,2,0:T(8,128)}, u32[]{:S(2)}, u32[]{:S(2)}) collective-permute-start(f32[2,128,2,128]{3,1,2,0:T(8,128)} %get-tuple-element.26), channel_id=1, source_target_pairs={{32,0},{36,4},{40,8},{44,12},{48,16},{52,20},{56,24},{60,28},{64,3... | collective-permute-start | bytes 786440 | tf_op jit(solution)/shard_map/ppermute | solution.py:12
  225.9 1.7 copy-start.6
  225.9 53.7 %collective-permute-start.14 = (f32[2,128,2,128]{3,1,2,0:T(8,128)S(1)}, f32[2,128,2,128]{3,1,2,0:T(8,128)}, u32[]{:S(2)}, u32[]{:S(2)}) collective-permute-start(f32[2,128,2,128]{3,1,2,0:T(8,128)S(1)} %get-tuple-element.27), channel_id=1, source_target_pairs={{28,0},{32,4},{36,8},{40,12},{44,16},{48,20},{52,24},{56,28},{60,3... | collective-permute-start | bytes 786440 | tf_op jit(solution)/shard_map/ppermute | solution.py:12
Sparse Core Ops, SparseCore 0:
  11.6 138.5 all-gather.5
  152.0 22.0 all-gather.3
  184.5 37.0 reduce-scatter.2
  224.1 419.5 reduce-scatter.4

commit v2 on v1

--- a/solution.py
+++ b/solution.py
@@ -72,8 +72,11 @@
         attended_output,
         preferred_element_type=jnp.float32,
     )
-    proj_summed = lax.psum_scatter(proj_partial, "ctx", scatter_dimension=0, tiled=True)
-    grad_proj = proj_summed.reshape(proj_rows, -1) * (ctx_count * tok_rows) ** (-0.5)
+    proj_pieces = lax.all_to_all(
+        proj_partial.astype(jnp.bfloat16), "ctx", split_axis=0, concat_axis=0, tiled=True
+    )
+    proj_summed = jnp.sum(proj_pieces.astype(jnp.float32), axis=0)
+    grad_proj = proj_summed * (ctx_count * tok_rows) ** (-0.5)
     grouped_gradient = grad_attended.reshape(tok_rows, heads_kv, group_size, head_size)
     attn_groups = attended_output.reshape(tok_rows, heads_kv, group_size, head_size)
     probability_gradient = jnp.einsum(

time: 659 us -> 415 us (0.63)
  waiting for transfers between devices: 540 us -> 291 us
  starting transfers between devices: 49.4 us -> 56.3 us
    reduce_scatter x1 -> x0, waiting for transfers between devices: 359 us -> none  [shards(): lax.psum_scatter(proj_partial, 'ctx', scatter_dimension=0, tiled=True)]
    ppermute x16, waiting for transfers between devices: 72.3 us -> 172 us  [passed_along(): return lax.ppermute(value, axis, pairs)]
    all_gather x1, waiting for transfers between devices: 92.4 us -> 118 us  [shards(): proj_full = lax.all_gather(out_proj, 'ctx', axis=0, tiled=True)]
    all_gather x1, waiting for transfers between devices: 15.1 us -> 0.02 us  [shards(): grad_full = lax.all_gather(out_grad, 'head', axis=1, tiled=True)]
    all_to_all x0 -> x1, starting transfers between devices: none -> 7.87 us  [shards(): lax.all_to_all(proj_partial.astype(jnp.bfloat16), 'ctx', split_axis=0, co...]
  transfers between devices with their start and end apart: 20 -> 20, of which waited for: 13 -> 7; matrix products, arithmetic and copies ran while one was open for 5% -> 6% of each run, Pallas kernels for 0% -> 0%
where the time goes in v2:
time: 415 us; the launch traced here: 413 us
  waiting for transfers between devices  291 us (70%)
  starting transfers between devices  56.3 us (14%)
  matrix products  21.3 us (5%)
  local copies, waits for them, and re-layouts  17.5 us (4%)
  between operations  14.2 us (3%)
  other arithmetic  12.4 us (3%)
    ppermute x16, waiting for transfers between devices, passed_along(): return lax.ppermute(value, axis, pairs)  172 us
    all_gather x1, waiting for transfers between devices, shards(): proj_full = lax.all_gather(out_proj, 'ctx', axis=0, tiled=True)  118 us
    ppermute x16, starting transfers between devices, passed_along(): return lax.ppermute(value, axis, pairs)  48.3 us
    unnamed x26, local copies, waits for them, and re-layouts  13.5 us
  transfers between devices with their start and end apart: 20, of which 7 were waited for; matrix products, arithmetic and copies ran while one was open for 6% of the time, Pallas kernels for 0%

profile of v2, /device:TPU:8, one launch (start us, length us, event | category | flops | bytes accessed | tf_op | source)
XLA Modules:
  0.0 413.0 jit_solution(11686386344148351027)
XLA Ops:
  8.0 0.7 all-gather.6.cloned.1.call-update
  8.7 0.9 copy_bitcast_fusion
  9.6 3.5 collective-permute-start.7
  13.1 4.2 %collective-permute-start.6 = (bf16[2,128,2,128]{3,1,2,0:T(8,128)(2,1)S(1)}, bf16[2,128,2,128]{3,1,2,0:T(8,128)(2,1)S(1)}, u32[]{:S(2)}, u32[]{:S(2)}) collective-permute-start(bf16[2,128,2,128]{3,1,2,0:T(8,128)(2,1)S(1)} %pad_maximum_fusion.1), channel_id=1, source_target_pairs={{0,8},{4,12},{8,16},{12,20},{16,24},{20,28},{24,32},{28,36},{32,40... | collective-permute-start | bytes 393224 | tf_op jit(solution)/shard_map/ppermute | solution.py:12
  17.3 4.3 %collective-permute-start.5 = (bf16[2,128,2,128]{3,1,2,0:T(8,128)(2,1)S(1)}, bf16[2,128,2,128]{3,1,2,0:T(8,128)(2,1)S(1)}, u32[]{:S(2)}, u32[]{:S(2)}) collective-permute-start(bf16[2,128,2,128]{3,1,2,0:T(8,128)(2,1)S(1)} %pad_maximum_fusion.1), channel_id=1, source_target_pairs={{0,12},{4,16},{8,20},{12,24},{16,28},{20,32},{24,36},{28,40},{32,4... | collective-permute-start | bytes 393224 | tf_op jit(solution)/shard_map/ppermute | solution.py:12
  21.6 6.0 %collective-permute-start.1 = (bf16[2,128,2,128]{3,1,2,0:T(8,128)(2,1)S(1)}, bf16[2,128,2,128]{3,1,2,0:T(8,128)(2,1)S(1)}, u32[]{:S(2)}, u32[]{:S(2)}) collective-permute-start(bf16[2,128,2,128]{3,1,2,0:T(8,128)(2,1)S(1)} %pad_maximum_fusion.1), channel_id=1, source_target_pairs={{0,28},{4,32},{8,36},{12,40},{16,44},{20,48},{24,52},{28,56},{32,6... | collective-permute-start | bytes 393224 | tf_op jit(solution)/shard_map/ppermute | solution.py:12
  27.6 5.5 %collective-permute-start = (bf16[2,128,2,128]{3,1,2,0:T(8,128)(2,1)S(1)}, bf16[2,128,2,128]{3,1,2,0:T(8,128)(2,1)S(1)}, u32[]{:S(2)}, u32[]{:S(2)}) collective-permute-start(bf16[2,128,2,128]{3,1,2,0:T(8,128)(2,1)S(1)} %pad_maximum_fusion.1), channel_id=1, source_target_pairs={{0,32},{4,36},{8,40},{12,44},{16,48},{20,52},{24,56},{28,60},{32,6... | collective-permute-start | bytes 393224 | tf_op jit(solution)/shard_map/ppermute | solution.py:12
  33.1 0.8 dynamic_slice.6
  33.9 0.8 pad_dynamic-slice_fusion
  34.7 1.0 fusion.15
  35.7 1.6 collective-permute-done
  37.3 5.1 %collective-permute-start.2 = (bf16[2,128,2,128]{3,1,2,0:T(8,128)(2,1)S(1)}, bf16[2,128,2,128]{3,1,2,0:T(8,128)(2,1)S(1)}, u32[]{:S(2)}, u32[]{:S(2)}) collective-permute-start(bf16[2,128,2,128]{3,1,2,0:T(8,128)(2,1)S(1)} %pad_maximum_fusion.1), channel_id=1, source_target_pairs={{0,24},{4,28},{8,32},{12,36},{16,40},{20,44},{24,48},{28,52},{32,5... | collective-permute-start | bytes 393224 | tf_op jit(solution)/shard_map/ppermute | solution.py:12
  42.5 3.7 collective-permute-start.3
  46.2 4.4 %collective-permute-start.4 = (bf16[2,128,2,128]{3,1,2,0:T(8,128)(2,1)S(1)}, bf16[2,128,2,128]{3,1,2,0:T(8,128)(2,1)S(1)}, u32[]{:S(2)}, u32[]{:S(2)}) collective-permute-start(bf16[2,128,2,128]{3,1,2,0:T(8,128)(2,1)S(1)} %pad_maximum_fusion.1), channel_id=1, source_target_pairs={{0,16},{4,20},{8,24},{12,28},{16,32},{20,36},{24,40},{28,44},{32,4... | collective-permute-start | bytes 393224 | tf_op jit(solution)/shard_map/ppermute | solution.py:12
  50.7 2.4 collective-permute-done.4
  53.3 2.5 fusion.42
  55.9 1.9 fusion.12
  57.8 2.2 reshape.48
  60.0 118.1 %all-gather.6.cloned.1.call-done = bf16[64,84,512]{2,1,0:T(8,128)(2,1)} async-done(((bf16[1,84,512]{2,1,0:T(8,128)(2,1)}), bf16[64,84,512]{2,1,0:T(8,128)(2,1)}) %all-gather.6.cloned.1.call-update) | async-done | bytes 5505040 | tf_op jit(solution)/shard_map/all_gather | solution.py:57
  178.1 8.9 %reshape.50 = bf16[5376,512]{1,0:T(8,128)(2,1)} reshape(bf16[64,84,512]{2,1,0:T(8,128)(2,1)} %all-gather.6.cloned.1.call-done) | data formatting | bytes 11010048
  187.0 3.9 convolution_convert_fusion
  191.1 1.5 multiply_reduce_fusion
  192.6 4.2 %convert_bitcast_fusion = bf16[64,84,512]{2,1,0:T(8,128)(2,1)} fusion(bf16[128,512,1]{0,1,2:T(8,128)(2,1)S(1)} %bitcast.105, bf16[128,64,84]{0,2,1:T(8,128)(2,1)S(1)} %reshape.48), kind=kOutput, calls=%fused_computation.2 | convolution fusion | flops 707395584 | bytes 7012352 | tf_op jit(solution)/shard_map/tcr,tj->crj/dot_general | solution.py:69
  196.8 7.9 %all-to-all-start = ((bf16[64,84,512]{2,1,0:T(8,128)(2,1)}), bf16[64,84,512]{2,1,0:T(8,128)(2,1)}, u32[]{:S(2)}, u32[]{:S(2)}) async-start(bf16[64,84,512]{2,1,0:T(8,128)(2,1)} %convert_bitcast_fusion), calls=%async_computation.1 | async-start | bytes 11534336 | tf_op jit(solution)/shard_map/all_to_all | solution.py:75
  204.7 5.7 %fusion.45 = f32[128,5376]{0,1:T(8,128)} fusion(bf16[5376,512]{1,0:T(8,128)(2,1)} %reshape.50, bf16[128,512]{0,1:T(8,128)(2,1)S(1)} %bitcast.106), kind=kOutput, calls=%fused_computation.90 | convolution fusion | flops 704643072 | bytes 8388608 | tf_op jit(solution)/shard_map/dot_general | solution.py:58
  210.4 1.2 copy-done.4
  211.7 2.1 fusion.8
  214.8 1.1 fusion.26
  216.1 2.5 collective-permute-start.8
  218.7 1.3 collective-permute-start.9
  220.0 1.3 collective-permute-start.10
  221.3 1.3 collective-permute-start.11
  222.6 1.3 collective-permute-start.12
  223.9 19.3 %collective-permute-done.8 = f32[2,128,2,128]{3,1,2,0:T(8,128)S(1)} collective-permute-done((f32[2,128,2,128]{3,1,2,0:T(8,128)S(1)}, f32[2,128,2,128]{3,1,2,0:T(8,128)S(1)}, u32[]{:S(2)}, u32[]{:S(2)}) %collective-permute-start.8) | collective-permute-done | bytes 262176 | tf_op jit(solution)/shard_map/ppermute | solution.py:12
  243.2 1.3 collective-permute-start.13
  244.4 1.3 collective-permute-start.15
  245.7 103.3 %collective-permute-done.10 = f32[2,128,2,128]{3,1,2,0:T(8,128)S(1)} collective-permute-done((f32[2,128,2,128]{3,1,2,0:T(8,128)S(1)}, f32[2,128,2,128]{3,1,2,0:T(8,128)S(1)}, u32[]{:S(2)}, u32[]{:S(2)}) %collective-permute-start.10) | collective-permute-done | bytes 262176 | tf_op jit(solution)/shard_map/ppermute | solution.py:12
  349.1 0.7 copy-done.6
  349.8 1.3 collective-permute-start.14
  351.5 0.8 copy.56
  352.3 28.4 %collective-permute-done.15 = f32[2,128,2,128]{3,1,2,0:T(8,128)} collective-permute-done((f32[2,128,2,128]{3,1,2,0:T(8,128)}, f32[2,128,2,128]{3,1,2,0:T(8,128)}, u32[]{:S(2)}, u32[]{:S(2)}) %collective-permute-start.15) | collective-permute-done | bytes 262176 | tf_op jit(solution)/shard_map/ppermute | solution.py:12
  380.6 16.9 %collective-permute-done.14 = f32[2,128,2,128]{3,1,2,0:T(8,128)} collective-permute-done((f32[2,128,2,128]{3,1,2,0:T(8,128)S(1)}, f32[2,128,2,128]{3,1,2,0:T(8,128)}, u32[]{:S(2)}, u32[]{:S(2)}) %collective-permute-start.14) | collective-permute-done | bytes 262176 | tf_op jit(solution)/shard_map/ppermute | solution.py:12
  397.5 1.5 fusion.32
  399.0 0.7 copy.58
  399.7 0.7 copy.57
  400.4 1.9 convert_element_type.50
  402.3 3.5 convert_reduce_fusion
  405.8 0.7 broadcast_multiply_fusion
  (47 shorter events, 2.8 us)
Async XLA Ops:
  7.2 46.1 %copy-start = (bf16[128,4,128]{2,1,0:T(4,128)(2,1)S(1)}, bf16[128,4,128]{2,1,0:T(4,128)(2,1)}, u32[]{:S(2)}) copy-start(bf16[128,4,128]{2,1,0:T(4,128)(2,1)} %param.6) | copy-start | bytes 393220
  7.2 50.6 %all-gather.4.cloned.1.call-start = ((), (), s32[]{:S(2)}) async-start(), calls=%async_computation.3 | async-start | bytes 1720320 | tf_op jit(solution)/shard_map/all_gather | solution.py:64
  7.9 170.2 %all-gather.6.cloned.1.call-start = ((), (), s32[]{:S(2)}) async-start(), calls=%async_computation.4 | async-start | bytes 5857280 | tf_op jit(solution)/shard_map/all_gather | solution.py:57
  9.6 43.7 %collective-permute-start.7 = (bf16[2,128,2,128]{3,1,2,0:T(8,128)(2,1)S(1)}, bf16[2,128,2,128]{3,1,2,0:T(8,128)(2,1)S(1)}, u32[]{:S(2)}, u32[]{:S(2)}) collective-permute-start(bf16[2,128,2,128]{3,1,2,0:T(8,128)(2,1)S(1)} %pad_maximum_fusion.1), channel_id=1, source_target_pairs={{0,4},{4,8},{8,12},{12,16},{16,20},{20,24},{24,28},{28,32},{32,36}... | collective-permute-start | bytes 393224 | tf_op jit(solution)/shard_map/ppermute | solution.py:12
  13.1 40.1 %collective-permute-start.6 = (bf16[2,128,2,128]{3,1,2,0:T(8,128)(2,1)S(1)}, bf16[2,128,2,128]{3,1,2,0:T(8,128)(2,1)S(1)}, u32[]{:S(2)}, u32[]{:S(2)}) collective-permute-start(bf16[2,128,2,128]{3,1,2,0:T(8,128)(2,1)S(1)} %pad_maximum_fusion.1), channel_id=1, source_target_pairs={{0,8},{4,12},{8,16},{12,20},{16,24},{20,28},{24,32},{28,36},{32,40... | collective-permute-start | bytes 393224 | tf_op jit(solution)/shard_map/ppermute | solution.py:12
  17.3 35.9 %collective-permute-start.5 = (bf16[2,128,2,128]{3,1,2,0:T(8,128)(2,1)S(1)}, bf16[2,128,2,128]{3,1,2,0:T(8,128)(2,1)S(1)}, u32[]{:S(2)}, u32[]{:S(2)}) collective-permute-start(bf16[2,128,2,128]{3,1,2,0:T(8,128)(2,1)S(1)} %pad_maximum_fusion.1), channel_id=1, source_target_pairs={{0,12},{4,16},{8,20},{12,24},{16,28},{20,32},{24,36},{28,40},{32,4... | collective-permute-start | bytes 393224 | tf_op jit(solution)/shard_map/ppermute | solution.py:12
  21.6 20.8 %collective-permute-start.1 = (bf16[2,128,2,128]{3,1,2,0:T(8,128)(2,1)S(1)}, bf16[2,128,2,128]{3,1,2,0:T(8,128)(2,1)S(1)}, u32[]{:S(2)}, u32[]{:S(2)}) collective-permute-start(bf16[2,128,2,128]{3,1,2,0:T(8,128)(2,1)S(1)} %pad_maximum_fusion.1), channel_id=1, source_target_pairs={{0,28},{4,32},{8,36},{12,40},{16,44},{20,48},{24,52},{28,56},{32,6... | collective-permute-start | bytes 393224 | tf_op jit(solution)/shard_map/ppermute | solution.py:12
  27.6 9.7 %collective-permute-start = (bf16[2,128,2,128]{3,1,2,0:T(8,128)(2,1)S(1)}, bf16[2,128,2,128]{3,1,2,0:T(8,128)(2,1)S(1)}, u32[]{:S(2)}, u32[]{:S(2)}) collective-permute-start(bf16[2,128,2,128]{3,1,2,0:T(8,128)(2,1)S(1)} %pad_maximum_fusion.1), channel_id=1, source_target_pairs={{0,32},{4,36},{8,40},{12,44},{16,48},{20,52},{24,56},{28,60},{32,6... | collective-permute-start | bytes 393224 | tf_op jit(solution)/shard_map/ppermute | solution.py:12
  37.3 8.9 %collective-permute-start.2 = (bf16[2,128,2,128]{3,1,2,0:T(8,128)(2,1)S(1)}, bf16[2,128,2,128]{3,1,2,0:T(8,128)(2,1)S(1)}, u32[]{:S(2)}, u32[]{:S(2)}) collective-permute-start(bf16[2,128,2,128]{3,1,2,0:T(8,128)(2,1)S(1)} %pad_maximum_fusion.1), channel_id=1, source_target_pairs={{0,24},{4,28},{8,32},{12,36},{16,40},{20,44},{24,48},{28,52},{32,5... | collective-permute-start | bytes 393224 | tf_op jit(solution)/shard_map/ppermute | solution.py:12
  42.5 8.2 %collective-permute-start.3 = (bf16[2,128,2,128]{3,1,2,0:T(8,128)(2,1)S(1)}, bf16[2,128,2,128]{3,1,2,0:T(8,128)(2,1)S(1)}, u32[]{:S(2)}, u32[]{:S(2)}) collective-permute-start(bf16[2,128,2,128]{3,1,2,0:T(8,128)(2,1)S(1)} %pad_maximum_fusion.1), channel_id=1, source_target_pairs={{0,20},{4,24},{8,28},{12,32},{16,36},{20,40},{24,44},{28,48},{32,5... | collective-permute-start | bytes 393224 | tf_op jit(solution)/shard_map/ppermute | solution.py:12
  46.2 6.9 %collective-permute-start.4 = (bf16[2,128,2,128]{3,1,2,0:T(8,128)(2,1)S(1)}, bf16[2,128,2,128]{3,1,2,0:T(8,128)(2,1)S(1)}, u32[]{:S(2)}, u32[]{:S(2)}) collective-permute-start(bf16[2,128,2,128]{3,1,2,0:T(8,128)(2,1)S(1)} %pad_maximum_fusion.1), channel_id=1, source_target_pairs={{0,16},{4,20},{8,24},{12,28},{16,32},{20,36},{24,40},{28,44},{32,4... | collective-permute-start | bytes 393224 | tf_op jit(solution)/shard_map/ppermute | solution.py:12
  53.3 2.5 copy-start.3
  196.8 205.5 %all-to-all-start = ((bf16[64,84,512]{2,1,0:T(8,128)(2,1)}), bf16[64,84,512]{2,1,0:T(8,128)(2,1)}, u32[]{:S(2)}, u32[]{:S(2)}) async-start(bf16[64,84,512]{2,1,0:T(8,128)(2,1)} %convert_bitcast_fusion), calls=%async_computation.1 | async-start | bytes 11534336 | tf_op jit(solution)/shard_map/all_to_all | solution.py:75
  204.6 195.8 %reduce-scatter.2.cloned.1.call-start = ((), (), s32[]{:S(2)}) async-start(), calls=%async_computation.2 | async-start | bytes 3440640 | tf_op jit(solution)/shard_map/reduce_scatter | solution.py:61
  210.4 1.3 copy-start.4
  214.7 1.4 copy-start.1
  214.8 136.3 %copy-start.5 = (bf16[2,1152,2,128]{3,1,2,0:T(8,128)(2,1)S(1)}, bf16[2,1152,2,128]{3,1,2,0:T(8,128)(2,1)}, u32[]{:S(2)}) copy-start(bf16[2,1152,2,128]{3,1,2,0:T(8,128)(2,1)} %copy-done.3) | copy-start | bytes 3538948
  216.1 181.4 %copy-start.2 = (f32[1,1152,2,128]{3,1,2,0:T(8,128)S(1)}, f32[1,1152,2,128]{3,1,2,0:T(8,128)}, u32[]{:S(2)}) copy-start(f32[1,1152,2,128]{3,1,2,0:T(8,128)} %copy-done.1) | copy-start | bytes 3538948
  216.1 27.0 %collective-permute-start.8 = (f32[2,128,2,128]{3,1,2,0:T(8,128)S(1)}, f32[2,128,2,128]{3,1,2,0:T(8,128)S(1)}, u32[]{:S(2)}, u32[]{:S(2)}) collective-permute-start(f32[2,128,2,128]{3,1,2,0:T(8,128)S(1)} %get-tuple-element.20), channel_id=1, source_target_pairs={{4,0},{8,4},{12,8},{16,12},{20,16},{24,20},{28,24},{32,28},{36,32}... | collective-permute-start | bytes 786440 | tf_op jit(solution)/shard_map/ppermute | solution.py:12
  218.7 25.8 %collective-permute-start.9 = (f32[2,128,2,128]{3,1,2,0:T(8,128)S(1)}, f32[2,128,2,128]{3,1,2,0:T(8,128)S(1)}, u32[]{:S(2)}, u32[]{:S(2)}) collective-permute-start(f32[2,128,2,128]{3,1,2,0:T(8,128)S(1)} %get-tuple-element.21), channel_id=1, source_target_pairs={{8,0},{12,4},{16,8},{20,12},{24,16},{28,20},{32,24},{36,28},{40,32... | collective-permute-start | bytes 786440 | tf_op jit(solution)/shard_map/ppermute | solution.py:12
  220.0 129.1 %collective-permute-start.10 = (f32[2,128,2,128]{3,1,2,0:T(8,128)S(1)}, f32[2,128,2,128]{3,1,2,0:T(8,128)S(1)}, u32[]{:S(2)}, u32[]{:S(2)}) collective-permute-start(f32[2,128,2,128]{3,1,2,0:T(8,128)S(1)} %get-tuple-element.22), channel_id=1, source_target_pairs={{12,0},{16,4},{20,8},{24,12},{28,16},{32,20},{36,24},{40,28},{44,3... | collective-permute-start | bytes 786440 | tf_op jit(solution)/shard_map/ppermute | solution.py:12
  221.3 131.0 %collective-permute-start.11 = (f32[2,128,2,128]{3,1,2,0:T(8,128)}, f32[2,128,2,128]{3,1,2,0:T(8,128)}, u32[]{:S(2)}, u32[]{:S(2)}) collective-permute-start(f32[2,128,2,128]{3,1,2,0:T(8,128)} %get-tuple-element.23), channel_id=1, source_target_pairs={{16,0},{20,4},{24,8},{28,12},{32,16},{36,20},{40,24},{44,28},{48,3... | collective-permute-start | bytes 786440 | tf_op jit(solution)/shard_map/ppermute | solution.py:12
  222.6 129.7 %collective-permute-start.12 = (f32[2,128,2,128]{3,1,2,0:T(8,128)}, f32[2,128,2,128]{3,1,2,0:T(8,128)}, u32[]{:S(2)}, u32[]{:S(2)}) collective-permute-start(f32[2,128,2,128]{3,1,2,0:T(8,128)} %get-tuple-element.24), channel_id=1, source_target_pairs={{20,0},{24,4},{28,8},{32,12},{36,16},{40,20},{44,24},{48,28},{52,3... | collective-permute-start | bytes 786440 | tf_op jit(solution)/shard_map/ppermute | solution.py:12
  243.2 109.1 %collective-permute-start.13 = (f32[2,128,2,128]{3,1,2,0:T(8,128)}, f32[2,128,2,128]{3,1,2,0:T(8,128)}, u32[]{:S(2)}, u32[]{:S(2)}) collective-permute-start(f32[2,128,2,128]{3,1,2,0:T(8,128)} %get-tuple-element.25), channel_id=1, source_target_pairs={{24,0},{28,4},{32,8},{36,12},{40,16},{44,20},{48,24},{52,28},{56,3... | collective-permute-start | bytes 786440 | tf_op jit(solution)/shard_map/ppermute | solution.py:12
  244.4 136.2 %collective-permute-start.15 = (f32[2,128,2,128]{3,1,2,0:T(8,128)}, f32[2,128,2,128]{3,1,2,0:T(8,128)}, u32[]{:S(2)}, u32[]{:S(2)}) collective-permute-start(f32[2,128,2,128]{3,1,2,0:T(8,128)} %get-tuple-element.26), channel_id=1, source_target_pairs={{32,0},{36,4},{40,8},{44,12},{48,16},{52,20},{56,24},{60,28},{64,3... | collective-permute-start | bytes 786440 | tf_op jit(solution)/shard_map/ppermute | solution.py:12
  349.1 0.7 copy-start.6
  349.8 47.7 %collective-permute-start.14 = (f32[2,128,2,128]{3,1,2,0:T(8,128)S(1)}, f32[2,128,2,128]{3,1,2,0:T(8,128)}, u32[]{:S(2)}, u32[]{:S(2)}) collective-permute-start(f32[2,128,2,128]{3,1,2,0:T(8,128)S(1)} %get-tuple-element.27), channel_id=1, source_target_pairs={{28,0},{32,4},{36,8},{40,12},{44,16},{48,20},{52,24},{56,28},{60,3... | collective-permute-start | bytes 786440 | tf_op jit(solution)/shard_map/ppermute | solution.py:12
Sparse Core Ops, SparseCore 0:
  9.8 35.4 all-gather.3
  48.9 129.2 all-gather.5
  210.5 49.3 reduce-scatter.1

commit v3 on v0

--- a/solution.py
+++ b/solution.py
@@ -54,6 +54,16 @@
     attended_output = attended_output.astype(jnp.bfloat16).reshape(
         tok_rows, heads_query * head_size
     )
+    grad_full = lax.all_gather(out_grad, "head", axis=1, tiled=True)
+    proj_rows = grad_full.shape[1] // ctx_count
+    proj_partial = jnp.einsum(
+        "tcr,tj->crj",
+        grad_full.reshape(tok_rows, ctx_count, proj_rows),
+        attended_output,
+        preferred_element_type=jnp.float32,
+    ).astype(jnp.bfloat16)
+    proj_partial, out_proj = lax.optimization_barrier((proj_partial, out_proj))
+    proj_pieces = lax.all_to_all(proj_partial, "ctx", split_axis=0, concat_axis=0, tiled=True)
     proj_full = lax.all_gather(out_proj, "ctx", axis=0, tiled=True)
     out_partial = lax.dot_general(
         attended_output, proj_full, (((1,), (1,)), ((), ())), preferred_element_type=jnp.float32
@@ -61,18 +71,10 @@
     layer_out = lax.psum_scatter(out_partial, "head", scatter_dimension=1, tiled=True).astype(
         jnp.bfloat16
     )
-    grad_full = lax.all_gather(out_grad, "head", axis=1, tiled=True)
     grad_attended = jnp.dot(grad_full, proj_full, preferred_element_type=jnp.float32).astype(
         jnp.bfloat16
     )
-    proj_summed = lax.psum_scatter(
-        lax.dot_general(
-            grad_full, attended_output, (((0,), (0,)), ((), ())), preferred_element_type=jnp.float32
-        ),
-        "ctx",
-        scatter_dimension=0,
-        tiled=True,
-    )
+    proj_summed = jnp.sum(proj_pieces.astype(jnp.float32), axis=0)
     grad_proj = proj_summed * (ctx_count * tok_rows) ** (-0.5)
     grouped_gradient = grad_attended.reshape(tok_rows, heads_kv, group_size, head_size)
     attn_groups = attended_output.reshape(tok_rows, heads_kv, group_size, head_size)
@@ -100,7 +102,9 @@
     for offset in range(blocks):
         distance = offset + 1
         portion = halo_part[:, (blocks - distance) * tok_rows : (blocks - distance + 1) * tok_rows]
-        summed = summed + passed_along(portion, "ctx", -distance)
+        summed = summed + passed_along(portion.astype(jnp.bfloat16), "ctx", -distance).astype(
+            jnp.float32
+        )
     grad_key = summed[0].astype(jnp.bfloat16)
     grad_value = summed[1].astype(jnp.bfloat16)
     return (layer_out, query_gradient, grad_key, grad_value, grad_proj)

time: 1000 us -> 328 us (0.33)
  the two profiles are of different devices: /device:TPU:8 before, /device:TPU:229 now
where the time goes in v3:
time: 328 us; the launch traced here: 327 us
  waiting for transfers between devices  204 us (62%)
  starting transfers between devices  60 us (18%)
  local copies, waits for them, and re-layouts  21.4 us (7%)
  matrix products  18.7 us (6%)
  between operations  14.2 us (4%)
  other arithmetic  8.44 us (3%)
    all_gather x1, waiting for transfers between devices, shards(): proj_full = lax.all_gather(out_proj, 'ctx', axis=0, tiled=True)  164 us
    ppermute x16, starting transfers between devices, passed_along(): return lax.ppermute(value, axis, pairs)  45.9 us
    ppermute x16, waiting for transfers between devices, passed_along(): return lax.ppermute(value, axis, pairs)  28.4 us
    unnamed x30, local copies, waits for them, and re-layouts  16.6 us
    all_to_all x1, starting transfers between devices, shards(): lax.all_to_all(proj_partial, 'ctx', split_axis=0, concat_axis=0, tiled=True)  14 us
    reduce_scatter x1, waiting for transfers between devices, shards(): lax.psum_scatter(out_partial, 'head', scatter_dimension=1, tiled=True)  12 us
  transfers between devices with their start and end apart: 20, of which 7 were waited for; matrix products, arithmetic and copies ran while one was open for 10% of the time, Pallas kernels for 0%

profile of v3, /device:TPU:229, one launch (start us, length us, event | category | flops | bytes accessed | tf_op | source)
XLA Modules:
  0.0 327.0 jit_solution(4126129268754670511)
XLA Ops:
  7.2 0.9 copy_bitcast_fusion
  8.2 3.2 collective-permute-start.7
  11.4 4.5 %collective-permute-start.6 = (bf16[2,128,2,128]{3,1,2,0:T(8,128)(2,1)S(1)}, bf16[2,128,2,128]{3,1,2,0:T(8,128)(2,1)S(1)}, u32[]{:S(2)}, u32[]{:S(2)}) collective-permute-start(bf16[2,128,2,128]{3,1,2,0:T(8,128)(2,1)S(1)} %pad_maximum_fusion.1), channel_id=1, source_target_pairs={{0,8},{4,12},{8,16},{12,20},{16,24},{20,28},{24,32},{28,36},{32,40... | collective-permute-start | bytes 393224 | tf_op jit(solution)/shard_map/ppermute | solution.py:12
  15.9 1.9 collective-permute-start.5
  17.9 1.3 collective-permute-start.1
  19.2 1.3 collective-permute-start
  20.6 0.8 dynamic_slice.6
  21.3 0.8 pad_dynamic-slice_fusion
  22.1 1.0 fusion.16
  23.1 8.5 %collective-permute-done = bf16[2,128,2,128]{3,1,2,0:T(8,128)(2,1)S(1)} collective-permute-done((bf16[2,128,2,128]{3,1,2,0:T(8,128)(2,1)S(1)}, bf16[2,128,2,128]{3,1,2,0:T(8,128)(2,1)S(1)}, u32[]{:S(2)}, u32[]{:S(2)}) %collective-permute-start) | collective-permute-done | bytes 131104 | tf_op jit(solution)/shard_map/ppermute | solution.py:12
  31.7 1.3 collective-permute-start.2
  33.0 1.3 collective-permute-start.3
  34.3 9.1 %collective-permute-done.2 = bf16[2,128,2,128]{3,1,2,0:T(8,128)(2,1)S(1)} collective-permute-done((bf16[2,128,2,128]{3,1,2,0:T(8,128)(2,1)S(1)}, bf16[2,128,2,128]{3,1,2,0:T(8,128)(2,1)S(1)}, u32[]{:S(2)}, u32[]{:S(2)}) %collective-permute-start.2) | collective-permute-done | bytes 131104 | tf_op jit(solution)/shard_map/ppermute | solution.py:12
  43.5 1.3 collective-permute-start.4
  44.8 6.7 %collective-permute-done.3 = bf16[2,128,2,128]{3,1,2,0:T(8,128)(2,1)S(1)} collective-permute-done((bf16[2,128,2,128]{3,1,2,0:T(8,128)(2,1)S(1)}, bf16[2,128,2,128]{3,1,2,0:T(8,128)(2,1)S(1)}, u32[]{:S(2)}, u32[]{:S(2)}) %collective-permute-start.3) | collective-permute-done | bytes 131104 | tf_op jit(solution)/shard_map/ppermute | solution.py:12
  51.7 1.0 copy-done.5
  52.6 2.2 fusion.37
  55.0 1.3 copy-done.3
  56.3 1.0 copy-done.1
  57.7 2.2 reshape.46
  60.0 4.2 %convert_bitcast_fusion = bf16[64,84,512]{2,1,0:T(8,128)(2,1)} fusion(bf16[128,512,1]{0,1,2:T(8,128)(2,1)S(1)} %bitcast.105, bf16[128,64,84]{0,2,1:T(8,128)(2,1)S(1)} %reshape.46), kind=kOutput, calls=%fused_computation.2 | convolution fusion | flops 707395584 | bytes 7012352 | tf_op jit(solution)/shard_map/tcr,tj->crj/dot_general | solution.py:59
  64.2 14.0 %all-to-all-start = ((bf16[64,84,512]{2,1,0:T(8,128)(2,1)}), bf16[64,84,512]{2,1,0:T(8,128)(2,1)}, u32[]{:S(2)}, u32[]{:S(2)}) async-start(bf16[64,84,512]{2,1,0:T(8,128)(2,1)} %convert_bitcast_fusion), calls=%async_computation.1 | async-start | bytes 11534336 | tf_op jit(solution)/shard_map/all_to_all | solution.py:66
  78.2 163.8 %all-gather.6.cloned.1.call-done = bf16[64,84,512]{2,1,0:T(8,128)(2,1)} async-done(((bf16[1,84,512]{2,1,0:T(8,128)(2,1)}), bf16[64,84,512]{2,1,0:T(8,128)(2,1)}) %all-gather.6.cloned.1.call-update) | async-done | bytes 5505040 | tf_op jit(solution)/shard_map/all_gather | solution.py:67
  242.1 8.9 %reshape.50 = bf16[5376,512]{1,0:T(8,128)(2,1)} reshape(bf16[64,84,512]{2,1,0:T(8,128)(2,1)} %all-gather.6.cloned.1.call-done) | data formatting | bytes 11010048
  251.0 5.7 %fusion.40 = f32[128,5376]{0,1:T(8,128)} fusion(bf16[5376,512]{1,0:T(8,128)(2,1)} %reshape.50, bf16[128,512]{0,1:T(8,128)(2,1)S(1)} %bitcast.106), kind=kOutput, calls=%fused_computation.71 | convolution fusion | flops 704643072 | bytes 8388608 | tf_op jit(solution)/shard_map/dot_general | solution.py:68
  256.7 1.3 copy-done.8
  258.0 4.4 %multiply_reduce_fusion = (f32[128,2,2]{0,2,1:T(2,128)S(1)}, bf16[512,128]{1,0:T(8,128)(2,1)S(1)}) fusion(bf16[2,128,2,128]{3,1,2,0:T(8,128)(2,1)S(1)} %convolution_convert_fusion.1, bf16[5376,512]{1,0:T(8,128)(2,1)} %reshape.50, bf16[128,5376]{0,1:T(8,128)(2,1)S(1)} %copy-done.8), kind=kOutput, calls=%fused_computation.42 | convolution fusion | flops 704970240 | bytes 7145472 | tf_op jit(solution)/shard_map/dot_general | solution.py:74
  262.4 0.5 fusion.8
  263.3 0.8 copy.53
  264.1 0.5 fusion.10
  264.6 0.8 copy-done.2
  266.0 0.8 fusion.36
  266.9 2.1 collective-permute-start.8
  269.0 3.7 %collective-permute-start.15 = (bf16[2,128,2,128]{3,1,2,0:T(8,128)(2,1)}, bf16[2,128,2,128]{3,1,2,0:T(8,128)(2,1)S(1)}, u32[]{:S(2)}, u32[]{:S(2)}) collective-permute-start(bf16[2,128,2,128]{3,1,2,0:T(8,128)(2,1)} %get-tuple-element.25), channel_id=1, source_target_pairs={{32,0},{36,4},{40,8},{44,12},{48,16},{52,20},{56,24},{60,28},{64,3... | collective-permute-start | bytes 393224 | tf_op jit(solution)/shard_map/ppermute | solution.py:12
  272.7 5.2 %collective-permute-start.14 = (bf16[2,128,2,128]{3,1,2,0:T(8,128)(2,1)}, bf16[2,128,2,128]{3,1,2,0:T(8,128)(2,1)S(1)}, u32[]{:S(2)}, u32[]{:S(2)}) collective-permute-start(bf16[2,128,2,128]{3,1,2,0:T(8,128)(2,1)} %get-tuple-element.26), channel_id=1, source_target_pairs={{28,0},{32,4},{36,8},{40,12},{44,16},{48,20},{52,24},{56,28},{60,3... | collective-permute-start | bytes 393224 | tf_op jit(solution)/shard_map/ppermute | solution.py:12
  277.9 1.9 collective-permute-start.13
  279.8 4.4 %collective-permute-start.12 = (bf16[2,128,2,128]{3,1,2,0:T(8,128)(2,1)}, bf16[2,128,2,128]{3,1,2,0:T(8,128)(2,1)S(1)}, u32[]{:S(2)}, u32[]{:S(2)}) collective-permute-start(bf16[2,128,2,128]{3,1,2,0:T(8,128)(2,1)} %get-tuple-element.28), channel_id=1, source_target_pairs={{20,0},{24,4},{28,8},{32,12},{36,16},{40,20},{44,24},{48,28},{52,3... | collective-permute-start | bytes 393224 | tf_op jit(solution)/shard_map/ppermute | solution.py:12
  284.1 3.5 %convert_reduce_fusion = f32[84,512]{1,0:T(8,128)S(1)} fusion(bf16[64,84,512]{2,1,0:T(8,128)(2,1)} %all-to-all-done), kind=kLoop, calls=%fused_computation.1 | loop fusion | flops 5462016 | bytes 5677056 | tf_op jit(solution)/shard_map/reduce_sum | solution.py:77
  287.7 5.8 %collective-permute-start.11 = (bf16[2,128,2,128]{3,1,2,0:T(8,128)(2,1)S(1)}, bf16[2,128,2,128]{3,1,2,0:T(8,128)(2,1)S(1)}, u32[]{:S(2)}, u32[]{:S(2)}) collective-permute-start(bf16[2,128,2,128]{3,1,2,0:T(8,128)(2,1)S(1)} %get-tuple-element.29), channel_id=1, source_target_pairs={{16,0},{20,4},{24,8},{28,12},{32,16},{36,20},{40,24},{44,28},{48,3... | collective-permute-start | bytes 393224 | tf_op jit(solution)/shard_map/ppermute | solution.py:12
  293.5 2.7 collective-permute-start.10
  296.2 4.1 %collective-permute-start.9 = (bf16[2,128,2,128]{3,1,2,0:T(8,128)(2,1)S(1)}, bf16[2,128,2,128]{3,1,2,0:T(8,128)(2,1)S(1)}, u32[]{:S(2)}, u32[]{:S(2)}) collective-permute-start(bf16[2,128,2,128]{3,1,2,0:T(8,128)(2,1)S(1)} %get-tuple-element.31), channel_id=1, source_target_pairs={{8,0},{12,4},{16,8},{20,12},{24,16},{28,20},{32,24},{36,28},{40,32... | collective-permute-start | bytes 393224 | tf_op jit(solution)/shard_map/ppermute | solution.py:12
  300.2 0.7 broadcast_multiply_fusion
  300.9 0.7 collective-permute-done.10
  301.6 3.4 %collective-permute-done.9 = bf16[2,128,2,128]{3,1,2,0:T(8,128)(2,1)S(1)} collective-permute-done((bf16[2,128,2,128]{3,1,2,0:T(8,128)(2,1)S(1)}, bf16[2,128,2,128]{3,1,2,0:T(8,128)(2,1)S(1)}, u32[]{:S(2)}, u32[]{:S(2)}) %collective-permute-start.9) | collective-permute-done | bytes 131104 | tf_op jit(solution)/shard_map/ppermute | solution.py:12
  305.1 0.7 copy.55
  305.8 0.7 copy.54
  306.5 12.0 %reduce-scatter.2.cloned.1.call-done = f32[128,1344]{0,1:T(8,128)} async-done(((f32[128,5376]{0,1:T(8,128)}), f32[128,1344]{0,1:T(8,128)}) %reduce-scatter.2.cloned.1.call-update) | async-done | bytes 688144 | tf_op jit(solution)/shard_map/reduce_scatter | solution.py:71
  318.6 1.9 convert_element_type.87
  (51 shorter events, 2.2 us)
Async XLA Ops:
  7.2 45.5 %copy-start = (bf16[128,4,128]{2,1,0:T(4,128)(2,1)S(1)}, bf16[128,4,128]{2,1,0:T(4,128)(2,1)}, u32[]{:S(2)}) copy-start(bf16[128,4,128]{2,1,0:T(4,128)(2,1)} %param.6) | copy-start | bytes 393220
  7.2 50.5 %all-gather.4.cloned.1.call-start = ((), (), s32[]{:S(2)}) async-start(), calls=%async_computation.2 | async-start | bytes 1720320 | tf_op jit(solution)/shard_map/all_gather | solution.py:57
  8.2 43.4 %collective-permute-start.7 = (bf16[2,128,2,128]{3,1,2,0:T(8,128)(2,1)S(1)}, bf16[2,128,2,128]{3,1,2,0:T(8,128)(2,1)S(1)}, u32[]{:S(2)}, u32[]{:S(2)}) collective-permute-start(bf16[2,128,2,128]{3,1,2,0:T(8,128)(2,1)S(1)} %pad_maximum_fusion.1), channel_id=1, source_target_pairs={{0,4},{4,8},{8,12},{12,16},{16,20},{20,24},{24,28},{28,32},{32,36}... | collective-permute-start | bytes 393224 | tf_op jit(solution)/shard_map/ppermute | solution.py:12
  11.4 40.2 %collective-permute-start.6 = (bf16[2,128,2,128]{3,1,2,0:T(8,128)(2,1)S(1)}, bf16[2,128,2,128]{3,1,2,0:T(8,128)(2,1)S(1)}, u32[]{:S(2)}, u32[]{:S(2)}) collective-permute-start(bf16[2,128,2,128]{3,1,2,0:T(8,128)(2,1)S(1)} %pad_maximum_fusion.1), channel_id=1, source_target_pairs={{0,8},{4,12},{8,16},{12,20},{16,24},{20,28},{24,32},{28,36},{32,40... | collective-permute-start | bytes 393224 | tf_op jit(solution)/shard_map/ppermute | solution.py:12
  15.9 35.6 %collective-permute-start.5 = (bf16[2,128,2,128]{3,1,2,0:T(8,128)(2,1)S(1)}, bf16[2,128,2,128]{3,1,2,0:T(8,128)(2,1)S(1)}, u32[]{:S(2)}, u32[]{:S(2)}) collective-permute-start(bf16[2,128,2,128]{3,1,2,0:T(8,128)(2,1)S(1)} %pad_maximum_fusion.1), channel_id=1, source_target_pairs={{0,12},{4,16},{8,20},{12,24},{16,28},{20,32},{24,36},{28,40},{32,4... | collective-permute-start | bytes 393224 | tf_op jit(solution)/shard_map/ppermute | solution.py:12
  17.9 15.1 %collective-permute-start.1 = (bf16[2,128,2,128]{3,1,2,0:T(8,128)(2,1)S(1)}, bf16[2,128,2,128]{3,1,2,0:T(8,128)(2,1)S(1)}, u32[]{:S(2)}, u32[]{:S(2)}) collective-permute-start(bf16[2,128,2,128]{3,1,2,0:T(8,128)(2,1)S(1)} %pad_maximum_fusion.1), channel_id=1, source_target_pairs={{0,28},{4,32},{8,36},{12,40},{16,44},{20,48},{24,52},{28,56},{32,6... | collective-permute-start | bytes 393224 | tf_op jit(solution)/shard_map/ppermute | solution.py:12
  19.2 12.5 %collective-permute-start = (bf16[2,128,2,128]{3,1,2,0:T(8,128)(2,1)S(1)}, bf16[2,128,2,128]{3,1,2,0:T(8,128)(2,1)S(1)}, u32[]{:S(2)}, u32[]{:S(2)}) collective-permute-start(bf16[2,128,2,128]{3,1,2,0:T(8,128)(2,1)S(1)} %pad_maximum_fusion.1), channel_id=1, source_target_pairs={{0,32},{4,36},{8,40},{12,44},{16,48},{20,52},{24,56},{28,60},{32,6... | collective-permute-start | bytes 393224 | tf_op jit(solution)/shard_map/ppermute | solution.py:12
  20.5 221.6 %all-gather.6.cloned.1.call-start = ((), (), s32[]{:S(2)}) async-start(), calls=%async_computation.4 | async-start | bytes 5857280 | tf_op jit(solution)/shard_map/all_gather | solution.py:67
  31.7 11.8 %collective-permute-start.2 = (bf16[2,128,2,128]{3,1,2,0:T(8,128)(2,1)S(1)}, bf16[2,128,2,128]{3,1,2,0:T(8,128)(2,1)S(1)}, u32[]{:S(2)}, u32[]{:S(2)}) collective-permute-start(bf16[2,128,2,128]{3,1,2,0:T(8,128)(2,1)S(1)} %pad_maximum_fusion.1), channel_id=1, source_target_pairs={{0,24},{4,28},{8,32},{12,36},{16,40},{20,44},{24,48},{28,52},{32,5... | collective-permute-start | bytes 393224 | tf_op jit(solution)/shard_map/ppermute | solution.py:12
  33.0 18.4 %collective-permute-start.3 = (bf16[2,128,2,128]{3,1,2,0:T(8,128)(2,1)S(1)}, bf16[2,128,2,128]{3,1,2,0:T(8,128)(2,1)S(1)}, u32[]{:S(2)}, u32[]{:S(2)}) collective-permute-start(bf16[2,128,2,128]{3,1,2,0:T(8,128)(2,1)S(1)} %pad_maximum_fusion.1), channel_id=1, source_target_pairs={{0,20},{4,24},{8,28},{12,32},{16,36},{20,40},{24,44},{28,48},{32,5... | collective-permute-start | bytes 393224 | tf_op jit(solution)/shard_map/ppermute | solution.py:12
  43.5 8.0 %collective-permute-start.4 = (bf16[2,128,2,128]{3,1,2,0:T(8,128)(2,1)S(1)}, bf16[2,128,2,128]{3,1,2,0:T(8,128)(2,1)S(1)}, u32[]{:S(2)}, u32[]{:S(2)}) collective-permute-start(bf16[2,128,2,128]{3,1,2,0:T(8,128)(2,1)S(1)} %pad_maximum_fusion.1), channel_id=1, source_target_pairs={{0,16},{4,20},{8,24},{12,28},{16,32},{20,36},{24,40},{28,44},{32,4... | collective-permute-start | bytes 393224 | tf_op jit(solution)/shard_map/ppermute | solution.py:12
  51.6 1.0 copy-start.5
  54.8 1.5 copy-start.3
  54.8 2.5 copy-start.6
  56.3 1.0 copy-start.1
  64.2 220.0 %all-to-all-start = ((bf16[64,84,512]{2,1,0:T(8,128)(2,1)}), bf16[64,84,512]{2,1,0:T(8,128)(2,1)}, u32[]{:S(2)}, u32[]{:S(2)}) async-start(bf16[64,84,512]{2,1,0:T(8,128)(2,1)} %convert_bitcast_fusion), calls=%async_computation.1 | async-start | bytes 11534336 | tf_op jit(solution)/shard_map/all_to_all | solution.py:66
  78.2 240.4 %reduce-scatter.2.cloned.1.call-start = ((), (), s32[]{:S(2)}) async-start(), calls=%async_computation.3 | async-start | bytes 3440640 | tf_op jit(solution)/shard_map/reduce_scatter | solution.py:71
  256.7 1.3 copy-start.8
  258.0 4.4 %copy-start.4 = (f32[2,2,128,1152]{2,3,1,0:T(8,128)S(1)}, f32[2,2,128,1152]{2,3,1,0:T(8,128)}, u32[]{:S(2)}) copy-start(f32[2,2,128,1152]{2,3,1,0:T(8,128)} %copy-done.3) | copy-start | bytes 7077892
  258.0 4.4 %copy-start.7 = (bf16[2,1152,2,128]{3,1,2,0:T(8,128)(2,1)S(1)}, bf16[2,1152,2,128]{3,1,2,0:T(8,128)(2,1)}, u32[]{:S(2)}) copy-start(bf16[2,1152,2,128]{3,1,2,0:T(8,128)(2,1)} %copy-done.5) | copy-start | bytes 3538948
  264.1 1.3 copy-start.2
  266.9 20.8 %collective-permute-start.8 = (bf16[2,128,2,128]{3,1,2,0:T(8,128)(2,1)}, bf16[2,128,2,128]{3,1,2,0:T(8,128)(2,1)S(1)}, u32[]{:S(2)}, u32[]{:S(2)}) collective-permute-start(bf16[2,128,2,128]{3,1,2,0:T(8,128)(2,1)} %get-tuple-element.24), channel_id=1, source_target_pairs={{4,0},{8,4},{12,8},{16,12},{20,16},{24,20},{28,24},{32,28},{36,32}... | collective-permute-start | bytes 393224 | tf_op jit(solution)/shard_map/ppermute | solution.py:12
  269.0 24.5 %collective-permute-start.15 = (bf16[2,128,2,128]{3,1,2,0:T(8,128)(2,1)}, bf16[2,128,2,128]{3,1,2,0:T(8,128)(2,1)S(1)}, u32[]{:S(2)}, u32[]{:S(2)}) collective-permute-start(bf16[2,128,2,128]{3,1,2,0:T(8,128)(2,1)} %get-tuple-element.25), channel_id=1, source_target_pairs={{32,0},{36,4},{40,8},{44,12},{48,16},{52,20},{56,24},{60,28},{64,3... | collective-permute-start | bytes 393224 | tf_op jit(solution)/shard_map/ppermute | solution.py:12
  272.7 23.5 %collective-permute-start.14 = (bf16[2,128,2,128]{3,1,2,0:T(8,128)(2,1)}, bf16[2,128,2,128]{3,1,2,0:T(8,128)(2,1)S(1)}, u32[]{:S(2)}, u32[]{:S(2)}) collective-permute-start(bf16[2,128,2,128]{3,1,2,0:T(8,128)(2,1)} %get-tuple-element.26), channel_id=1, source_target_pairs={{28,0},{32,4},{36,8},{40,12},{44,16},{48,20},{52,24},{56,28},{60,3... | collective-permute-start | bytes 393224 | tf_op jit(solution)/shard_map/ppermute | solution.py:12
  277.9 23.0 %collective-permute-start.13 = (bf16[2,128,2,128]{3,1,2,0:T(8,128)(2,1)}, bf16[2,128,2,128]{3,1,2,0:T(8,128)(2,1)S(1)}, u32[]{:S(2)}, u32[]{:S(2)}) collective-permute-start(bf16[2,128,2,128]{3,1,2,0:T(8,128)(2,1)} %get-tuple-element.27), channel_id=1, source_target_pairs={{24,0},{28,4},{32,8},{36,12},{40,16},{44,20},{48,24},{52,28},{56,3... | collective-permute-start | bytes 393224 | tf_op jit(solution)/shard_map/ppermute | solution.py:12
  279.8 21.2 %collective-permute-start.12 = (bf16[2,128,2,128]{3,1,2,0:T(8,128)(2,1)}, bf16[2,128,2,128]{3,1,2,0:T(8,128)(2,1)S(1)}, u32[]{:S(2)}, u32[]{:S(2)}) collective-permute-start(bf16[2,128,2,128]{3,1,2,0:T(8,128)(2,1)} %get-tuple-element.28), channel_id=1, source_target_pairs={{20,0},{24,4},{28,8},{32,12},{36,16},{40,20},{44,24},{48,28},{52,3... | collective-permute-start | bytes 393224 | tf_op jit(solution)/shard_map/ppermute | solution.py:12
  287.7 13.3 %collective-permute-start.11 = (bf16[2,128,2,128]{3,1,2,0:T(8,128)(2,1)S(1)}, bf16[2,128,2,128]{3,1,2,0:T(8,128)(2,1)S(1)}, u32[]{:S(2)}, u32[]{:S(2)}) collective-permute-start(bf16[2,128,2,128]{3,1,2,0:T(8,128)(2,1)S(1)} %get-tuple-element.29), channel_id=1, source_target_pairs={{16,0},{20,4},{24,8},{28,12},{32,16},{36,20},{40,24},{44,28},{48,3... | collective-permute-start | bytes 393224 | tf_op jit(solution)/shard_map/ppermute | solution.py:12
  293.5 8.1 %collective-permute-start.10 = (bf16[2,128,2,128]{3,1,2,0:T(8,128)(2,1)S(1)}, bf16[2,128,2,128]{3,1,2,0:T(8,128)(2,1)S(1)}, u32[]{:S(2)}, u32[]{:S(2)}) collective-permute-start(bf16[2,128,2,128]{3,1,2,0:T(8,128)(2,1)S(1)} %get-tuple-element.30), channel_id=1, source_target_pairs={{12,0},{16,4},{20,8},{24,12},{28,16},{32,20},{36,24},{40,28},{44,3... | collective-permute-start | bytes 393224 | tf_op jit(solution)/shard_map/ppermute | solution.py:12
  296.2 8.8 %collective-permute-start.9 = (bf16[2,128,2,128]{3,1,2,0:T(8,128)(2,1)S(1)}, bf16[2,128,2,128]{3,1,2,0:T(8,128)(2,1)S(1)}, u32[]{:S(2)}, u32[]{:S(2)}) collective-permute-start(bf16[2,128,2,128]{3,1,2,0:T(8,128)(2,1)S(1)} %get-tuple-element.31), channel_id=1, source_target_pairs={{8,0},{12,4},{16,8},{20,12},{24,16},{28,20},{32,24},{36,28},{40,32... | collective-permute-start | bytes 393224 | tf_op jit(solution)/shard_map/ppermute | solution.py:12
Sparse Core Ops, SparseCore 0:
  20.6 31.7 all-gather.3
  64.3 177.7 all-gather.5
  256.8 61.6 reduce-scatter.1
